TPU v7x, 128 devices: a whole 4x4x4 slice. The times are simulated.
128 devices in a mesh: expert: 32 (over y, z, core), ffn: 4 (over x).
Axes of the slice: x: 4, y: 4, z: 4, core: 2. Of those that a mesh axis runs over, the one named last changes fastest.
Arguments:
- tokens: bfloat16 [16384, 768], P('expert', 'ffn'), may hold values from -6 to 6
- cotangent: bfloat16 [16384, 768], P('expert', 'ffn'), may hold values from -6 to 6
- gates: float32 [16384, 2], P('expert'), may hold values from 0.2 to 1
- expert_ids: int32 [16384, 2], P('expert'), may hold values from 0 to 63, all different within a row; in each aligned block of 512 rows (0 to 511, 512 to 1023, ...) at most 32 rows name the same one
- up_weight: bfloat16 [64, 768, 3072], P('expert', None, 'ffn'), may hold values from -0.21875 to 0.21875
- down_weight: bfloat16 [64, 3072, 768], P('expert', 'ffn'), may hold values from -0.109375 to 0.109375
Outputs:
- layer_out: bfloat16 [16384, 768], P('expert', 'ffn')
- grad_tokens: bfloat16 [16384, 768], P('expert', 'ffn')
- grad_up: bfloat16 [64, 768, 3072], P('expert', None, 'ffn')
- grad_down: bfloat16 [64, 3072, 768], P('expert', 'ffn')
Inputs may be any that keep to these rules, and one draw needn't show every extreme that they name: `expert_ids`: the two experts of a token differ. Among the tokens of one index of expert no expert is named more than 32 times, a bound that some block reaches.
All inputs are finite; a program needn't handle non-finite values.
Results may differ from a plain program's by a relative error of at most 0.0065.
Values may be sent and summed in bfloat16 or wider, within the bound.
No kernel may reach another device: no remote copies, remote signals or barrier semaphores. Data moves between devices by JAX's collectives and lax.ppermute only.
A program may use at most 192 MiB of HBM per device.

v0:
```python
import jax
import jax.numpy as jnp
from jax import lax
from jax.experimental.layout import Layout, with_layout_constraint
from jax.sharding import PartitionSpec as P


def slot_targets(expert_ids, owners, local_experts, capacity):
    flat_ids = expert_ids.reshape(-1)
    count = flat_ids.shape[0]
    experts = owners * local_experts
    columns = lax.broadcasted_iota(jnp.int32, (count, experts), 1)
    onehot = (flat_ids[:, None] == columns).astype(jnp.bfloat16)
    earlier = (
        lax.broadcasted_iota(jnp.int32, (count, count), 0)
        > lax.broadcasted_iota(jnp.int32, (count, count), 1)
    ).astype(jnp.bfloat16)
    before = jnp.dot(earlier, onehot, preferred_element_type=jnp.float32)
    position = jnp.sum(onehot.astype(jnp.float32) * before, axis=1).astype(jnp.int32)
    return (
        flat_ids % local_experts * (owners * capacity)
        + flat_ids // local_experts * capacity
        + position
    )


def shards(tokens, cotangent, gates, expert_ids, up_weight, down_weight):
    owners = lax.axis_size("expert")
    local_experts = up_weight.shape[0]
    experts = owners * local_experts
    tok_rows = tokens.shape[0]
    capacity = 2 * tok_rows // owners
    rows = experts * capacity
    slots = owners * capacity
    target = slot_targets(expert_ids, owners, local_experts, capacity)
    row_ids = lax.broadcasted_iota(jnp.int32, (rows, 2 * tok_rows), 0)
    placer = (row_ids == target[None, :]).astype(jnp.bfloat16)
    tok_ids = lax.broadcasted_iota(jnp.int32, (rows, tok_rows), 0)
    pair = target.reshape(tok_rows, 2)
    token_placer = ((tok_ids == pair[None, :, 0]) | (tok_ids == pair[None, :, 1])).astype(
        jnp.bfloat16
    )
    weights = gates.reshape(-1)
    whole_tokens = lax.all_gather(tokens, "ffn", axis=1, tiled=True)
    whole_cot = lax.all_gather(cotangent, "ffn", axis=1, tiled=True)

    def dispatch(send):
        send = send.astype(jnp.bfloat16).reshape(local_experts, owners, capacity, send.shape[1])
        got = lax.all_to_all(send, "expert", split_axis=1, concat_axis=1, tiled=True)
        return got.reshape(local_experts, slots, got.shape[3])

    rows_in = dispatch(jnp.dot(token_placer, whole_tokens, preferred_element_type=jnp.float32))
    assigned = (weights[:, None] * jnp.repeat(whole_cot, 2, axis=0).astype(jnp.float32)).astype(
        jnp.bfloat16
    )
    grads_in = dispatch(jnp.dot(placer, assigned, preferred_element_type=jnp.float32))

    def send_home(parts):
        cols = jnp.stack(
            [
                lax.psum_scatter(
                    with_layout_constraint(part, Layout((0, 1))),
                    "ffn",
                    scatter_dimension=0,
                    tiled=True,
                )
                for part in parts
            ],
            axis=1,
        ).astype(jnp.bfloat16)
        cols = cols.reshape(cols.shape[0], local_experts, owners, capacity)
        back = lax.all_to_all(cols, "expert", split_axis=2, concat_axis=2, tiled=True)
        return back.reshape(back.shape[0], rows)

    preact = jnp.einsum("xsd,xdf->xsf", rows_in, up_weight, preferred_element_type=jnp.float32)
    gating = jax.nn.sigmoid(preact)
    activated = (preact * gating).astype(jnp.bfloat16)
    out_part = [
        jnp.einsum("fd,sf->ds", down_weight[x], activated[x], preferred_element_type=jnp.float32)
        for x in range(local_experts)
    ]
    out_home = send_home(out_part)
    back_grad = jnp.einsum(
        "xsd,xfd->xsf", grads_in, down_weight, preferred_element_type=jnp.float32
    )
    pre_grad = (back_grad * gating * (1.0 + preact * (1.0 - gating))).astype(jnp.bfloat16)
    grad_down = jnp.einsum(
        "xsf,xsd->xfd", activated, grads_in, preferred_element_type=jnp.float32
    ).astype(jnp.bfloat16)
    grad_up = jnp.einsum(
        "xsd,xsf->xdf", rows_in, pre_grad, preferred_element_type=jnp.float32
    ).astype(jnp.bfloat16)
    in_part = [
        jnp.einsum("df,sf->ds", up_weight[x], pre_grad[x], preferred_element_type=jnp.float32)
        for x in range(local_experts)
    ]
    in_home = send_home(in_part)

    def gather_back(returned):
        picked = lax.dot_general(
            placer, returned, (((0,), (1,)), ((), ())), preferred_element_type=jnp.float32
        )
        return picked.reshape(tok_rows, 2, returned.shape[0])

    layer_out = jnp.sum(gates[:, :, None] * gather_back(out_home), axis=1).astype(jnp.bfloat16)
    grad_tokens = jnp.sum(gather_back(in_home), axis=1).astype(jnp.bfloat16)
    return (layer_out, grad_tokens, grad_up, grad_down)


def solution(mesh):
    placed = (
        P("expert", "ffn"),
        P("expert", "ffn"),
        P("expert", None),
        P("expert", None),
        P("expert", None, "ffn"),
        P("expert", "ffn", None),
    )
    return jax.shard_map(
        shards,
        mesh=mesh,
        in_specs=placed,
        out_specs=(
            P("expert", "ffn"),
            P("expert", "ffn"),
            P("expert", None, "ffn"),
            P("expert", "ffn", None),
        ),
        check_vma=False,
    )
```

profile of v0, /device:TPU:1, one launch (start us, length us, event | category | flops | bytes accessed | tf_op | source)
XLA Modules:
  0.0 334.7 jit_solution(1738526114482320215)
XLA Ops:
  7.2 0.9 copy.55
  8.0 0.7 broadcast_compare_fusion
  8.7 0.2 reshape.148
  8.9 0.6 fusion.35
  9.5 0.2 convert_element_type.61
  9.7 0.2 copy.60
  9.9 0.3 fusion.38
  10.2 0.3 slice_reduce_fusion.1
  10.5 12.9 %all_gather.6 = bf16[512,768]{0,1:T(8,128)(2,1)S(1)} all-gather(bf16[512,192]{0,1:T(8,128)(2,1)S(1)} %copy-done.3), channel_id=1, replica_groups=mesh['expert'=32,'ffn'=4] {'ffn'}, dimensions={1}, use_global_device_ids=true | all-gather | bytes 983040 | tf_op jit(solution)/shard_map/all_gather | solution.py:44
  23.4 2.1 fusion.6
  25.5 1.9 copy.63
  27.4 10.5 %all-to-all-start = ((bf16[2,32,32,768]{3,2,0,1:T(8,128)(2,1)}), bf16[2,32,32,768]{3,2,0,1:T(8,128)(2,1)S(1)}, u32[]{:S(2)}, u32[]{:S(2)}) async-start(bf16[2,32,32,768]{3,2,0,1:T(8,128)(2,1)} %copy.63), calls=%async_computation | async-start | bytes 6291456 | tf_op jit(solution)/shard_map/all_to_all | solution.py:49
  37.9 13.0 %all_gather.7 = bf16[512,768]{0,1:T(8,128)(2,1)} all-gather(bf16[512,192]{0,1:T(8,128)(2,1)S(1)} %copy-done.4), channel_id=1, replica_groups=mesh['expert'=32,'ffn'=4] {'ffn'}, dimensions={1}, use_global_device_ids=true | all-gather | bytes 983040 | tf_op jit(solution)/shard_map/all_gather | solution.py:45
  50.9 2.5 copy.72
  53.5 4.2 %broadcast_in_dim.2 = f32[512,2,768]{2,1,0:T(2,128)} broadcast(f32[512,768]{1,0:T(8,128)} %copy.72), dimensions={0,2} | broadcast | bytes 4718592 | tf_op jit(solution)/shard_map/broadcast_in_dim | solution.py:53
  57.6 5.4 %convert_element_type.66 = f32[1024,768]{1,0:T(8,128)} reshape(f32[512,2,768]{2,1,0:T(2,128)} %broadcast_in_dim.2) | data formatting | bytes 6291456 | tf_op jit(solution)/shard_map/convert_element_type | solution.py:53
  63.0 0.1 copy.71
  63.1 0.2 mul.75
  63.3 6.0 %fusion.9 = bf16[2048,768]{1,0:T(8,128)(2,1)S(1)} fusion(s32[1024]{0:T(1024)S(1)} %fusion.48, f32[1024,768]{1,0:T(8,128)} %convert_element_type.66, f32[1024]{0:T(1024)S(1)} %mul.75), kind=kOutput, calls=%fused_computation.14 | convolution fusion | flops 3226468352 | bytes 6299648 | tf_op jit(solution)/shard_map/dot_general | solution.py:56
  69.4 2.0 copy.73
  71.4 6.3 %all-to-all-done = bf16[2,32,32,768]{3,2,0,1:T(8,128)(2,1)S(1)} async-done(((bf16[2,32,32,768]{3,2,0,1:T(8,128)(2,1)}), bf16[2,32,32,768]{3,2,0,1:T(8,128)(2,1)S(1)}, u32[]{:S(2)}, u32[]{:S(2)}) %all-to-all-start) | async-done | bytes 3145760 | tf_op jit(solution)/shard_map/all_to_all | solution.py:49
  77.7 5.1 %all-to-all-start.2 = ((bf16[2,32,32,768]{3,2,0,1:T(8,128)(2,1)}), bf16[2,32,32,768]{3,2,0,1:T(8,128)(2,1)}, u32[]{:S(2)}, u32[]{:S(2)}) async-start(bf16[2,32,32,768]{3,2,0,1:T(8,128)(2,1)} %copy.73), calls=%async_computation.4 | async-start | bytes 6291456 | tf_op jit(solution)/shard_map/all_to_all | solution.py:49
  82.7 0.2 reduce-scatter.9.cloned.1.call-start
  83.0 0.2 copy.64
  83.2 1.7 copy-done.2
  84.9 0.8 copy-done.6
  85.7 5.4 %multiply_convert_fusion.1 = (bf16[2,1024,768]{2,1,0:T(8,128)(2,1)}, f32[2,1024,768]{2,1,0:T(8,128)}) fusion(bf16[2,1024,768]{2,1,0:T(8,128)(2,1)S(1)} %bitcast.59, bf16[2,768,768]{2,1,0:T(8,128)(2,1)S(1)} %copy-done.6), kind=kOutput, calls=%fused_computation.4 | convolution fusion | flops 2423783424 | bytes 14942208 | tf_op jit(solution)/shard_map/xsd,xdf->xsf/dot_general | solution.py:75
  91.1 31.5 %all-to-all-done.2 = bf16[2,32,32,768]{3,2,0,1:T(8,128)(2,1)} async-done(((bf16[2,32,32,768]{3,2,0,1:T(8,128)(2,1)}), bf16[2,32,32,768]{3,2,0,1:T(8,128)(2,1)}, u32[]{:S(2)}, u32[]{:S(2)}) %all-to-all-start.2) | async-done | bytes 3145760 | tf_op jit(solution)/shard_map/all_to_all | solution.py:49
  122.7 2.3 copy.74
  124.9 0.3 copy-done.8
  125.3 6.6 %multiply_convert_fusion = bf16[2,1024,768]{2,1,0:T(8,128)(2,1)S(1)} fusion(f32[2,1024,768]{2,1,0:T(8,128)} %get-tuple-element.7, bf16[2,1024,768]{2,1,0:T(8,128)(2,1)S(1)} %bitcast.57, bf16[2,768,768]{2,1,0:T(8,128)(2,1)S(1)} %copy-done.8), kind=kOutput, calls=%fused_computation.3 | convolution fusion | flops 2430074880 | bytes 14942208 | tf_op jit(solution)/shard_map/xsd,xfd->xsf/dot_general | solution.py:83
  131.9 1.6 copy-done.10
  133.5 3.2 convolution_bitcast_fusion.1
  136.7 4.6 %convolution_bitcast_fusion = f32[768,1024]{1,0:T(8,128)} fusion(bf16[2,1024,768]{2,1,0:T(8,128)(2,1)} %copy-done.10, bf16[2,768,768]{2,1,0:T(8,128)(2,1)S(1)} %copy-done.7), kind=kOutput, calls=%fused_computation.24 | convolution fusion | flops 1207959552 | bytes 5898240 | tf_op jit(solution)/shard_map/df,sf->ds/dot_general | solution.py:94
  141.4 1.6 copy-done.9
  143.0 4.9 %convolution_bitcast_fusion.3 = f32[768,1024]{1,0:T(8,128)} fusion(bf16[2,1024,768]{2,1,0:T(8,128)(2,1)} %get-tuple-element.6, bf16[2,768,768]{2,1,0:T(8,128)(2,1)S(1)} %copy-done.9), kind=kOutput, calls=%fused_computation.27 | convolution fusion | flops 1207959552 | bytes 5898240 | tf_op jit(solution)/shard_map/fd,sf->ds/dot_general | solution.py:79
  148.0 4.5 %convolution_bitcast_fusion.2 = f32[768,1024]{1,0:T(8,128)} fusion(bf16[2,1024,768]{2,1,0:T(8,128)(2,1)} %get-tuple-element.6, bf16[2,768,768]{2,1,0:T(8,128)(2,1)S(1)} %copy-done.9), kind=kOutput, calls=%fused_computation.26 | convolution fusion | flops 1207959552 | bytes 5898240 | tf_op jit(solution)/shard_map/fd,sf->ds/dot_general | solution.py:79
  152.5 1.7 iota_compare_fusion.1
  154.2 7.8 %eq.58 = pred[512,2,2048]{2,1,0:T(4,128)(4,1)} reshape(pred[1024,2048]{1,0:T(8,128)(4,1)S(1)} %iota_compare_fusion.1) | data formatting | bytes 4194304 | tf_op jit(solution)/shard_map/eq | solution.py:37
  162.1 11.0 %reduce-scatter.9.cloned.1.call-done = f32[192,1024]{1,0:T(8,128)} async-done(((f32[768,1024]{1,0:T(8,128)}), f32[192,1024]{1,0:T(8,128)}) %reduce-scatter.9.cloned.1.call-update) | async-done | bytes 786448 | tf_op jit(solution)/shard_map/reduce_scatter | solution.py:61
  173.1 1.2 convert.18
  174.3 0.2 copy.75
  174.5 39.0 %reduce-scatter.11.cloned.1.call-done = f32[192,1024]{1,0:T(8,128)} async-done(((f32[768,1024]{1,0:T(8,128)}), f32[192,1024]{1,0:T(8,128)}) %reduce-scatter.11.cloned.1.call-update) | async-done | bytes 786448 | tf_op jit(solution)/shard_map/reduce_scatter | solution.py:61
  213.5 1.2 convert.19
  214.7 0.2 copy.76
  214.9 0.2 pad_maximum_fusion.1
  215.1 1.1 copy.77
  216.2 7.8 %all-to-all-start.3 = ((bf16[192,2,32,32]{0,3,1,2:T(8,128)(2,1)}), bf16[192,2,32,32]{0,3,1,2:T(8,128)(2,1)S(1)}, u32[]{:S(2)}, u32[]{:S(2)}) async-start(bf16[192,2,32,32]{0,3,1,2:T(8,128)(2,1)} %copy.77), calls=%async_computation.7 | async-start | bytes 2097152 | tf_op jit(solution)/shard_map/all_to_all | solution.py:72
  224.0 7.5 %convolution_convert_fusion.1 = bf16[2,768,768]{2,1,0:T(8,128)(2,1)} fusion(bf16[2,1024,768]{2,1,0:T(8,128)(2,1)} %bitcast.60, bf16[2,1024,768]{2,1,0:T(8,128)(2,1)} %copy-done.10), kind=kOutput, calls=%fused_computation.23 | convolution fusion | flops 2417098752 | bytes 8650752 | tf_op jit(solution)/shard_map/xsd,xsf->xdf/dot_general | solution.py:90
  231.4 22.5 %reduce-scatter.5.cloned.1.call-done = f32[192,1024]{1,0:T(8,128)} async-done(((f32[768,1024]{1,0:T(8,128)}), f32[192,1024]{1,0:T(8,128)}) %reduce-scatter.5.cloned.1.call-update) | async-done | bytes 786448 | tf_op jit(solution)/shard_map/reduce_scatter | solution.py:61
  254.0 1.2 convert.16
  255.1 0.2 copy.65
  255.3 38.9 %reduce-scatter.7.cloned.1.call-done = f32[192,1024]{1,0:T(8,128)} async-done(((f32[768,1024]{1,0:T(8,128)}), f32[192,1024]{1,0:T(8,128)}) %reduce-scatter.7.cloned.1.call-update) | async-done | bytes 786448 | tf_op jit(solution)/shard_map/reduce_scatter | solution.py:61
  294.2 1.2 convert.17
  295.4 0.2 copy.66
  295.6 0.2 pad_maximum_fusion
  295.9 1.1 copy.67
  297.0 7.8 %all-to-all-start.1 = ((bf16[192,2,32,32]{0,3,1,2:T(8,128)(2,1)}), bf16[192,2,32,32]{0,3,1,2:T(8,128)(2,1)S(1)}, u32[]{:S(2)}, u32[]{:S(2)}) async-start(bf16[192,2,32,32]{0,3,1,2:T(8,128)(2,1)} %copy.67), calls=%async_computation.3 | async-start | bytes 2097152 | tf_op jit(solution)/shard_map/all_to_all | solution.py:72
  304.7 7.1 %convolution_convert_fusion = bf16[2,768,768]{2,1,0:T(8,128)(2,1)} fusion(bf16[2,1024,768]{2,1,0:T(8,128)(2,1)} %get-tuple-element.6, bf16[2,1024,768]{2,1,0:T(8,128)(2,1)} %bitcast.58), kind=kOutput, calls=%fused_computation.22 | convolution fusion | flops 2417098752 | bytes 8650752 | tf_op jit(solution)/shard_map/xsf,xsd->xfd/dot_general | solution.py:87
  311.9 0.1 copy.78
  311.9 4.3 %fusion.23 = bf16[512,192]{0,1:T(8,128)(2,1)} fusion(bf16[192,2048,1]{0,1,2:T(8,128)(2,1)S(1)} %bitcast.68, pred[512,2,2048]{2,1,0:T(4,128)(4,1)S(1)} %copy-done), kind=kOutput, calls=%fused_computation.35 | convolution fusion | flops 805404672 | bytes 3080192 | tf_op jit(solution)/shard_map/dot_general | solution.py:100
  316.2 5.4 %all-to-all-done.1 = bf16[192,2,32,32]{0,3,1,2:T(8,128)(2,1)S(1)} async-done(((bf16[192,2,32,32]{0,3,1,2:T(8,128)(2,1)}), bf16[192,2,32,32]{0,3,1,2:T(8,128)(2,1)S(1)}, u32[]{:S(2)}, u32[]{:S(2)}) %all-to-all-start.1) | async-done | bytes 786464 | tf_op jit(solution)/shard_map/all_to_all | solution.py:72
  321.6 0.1 copy.68
  321.7 6.4 %fusion.20 = bf16[512,192]{0,1:T(8,128)(2,1)} fusion(bf16[192,2048,1]{0,1,2:T(8,128)(2,1)S(1)} %bitcast.67, pred[512,2,2048]{2,1,0:T(4,128)(4,1)} %eq.58, f32[512,2]{0,1:T(2,128)S(1)} %copy-done.5), kind=kOutput, calls=%fused_computation.34 | convolution fusion | flops 805601280 | bytes 3084288 | tf_op jit(solution)/shard_map/dot_general | solution.py:100
  (27 shorter events, 0.2 us)
Async XLA Ops:
  7.2 3.4 %copy-start.3 = (bf16[512,192]{0,1:T(8,128)(2,1)S(1)}, bf16[512,192]{0,1:T(8,128)(2,1)}, u32[]{:S(2)}) copy-start(bf16[512,192]{0,1:T(8,128)(2,1)} %param.6) | copy-start | bytes 589828
  27.4 10.5 %copy-start.4 = (bf16[512,192]{0,1:T(8,128)(2,1)S(1)}, bf16[512,192]{0,1:T(8,128)(2,1)}, u32[]{:S(2)}) copy-start(bf16[512,192]{0,1:T(8,128)(2,1)} %param.7) | copy-start | bytes 589828
  27.4 50.2 %all-to-all-start = ((bf16[2,32,32,768]{3,2,0,1:T(8,128)(2,1)}), bf16[2,32,32,768]{3,2,0,1:T(8,128)(2,1)S(1)}, u32[]{:S(2)}, u32[]{:S(2)}) async-start(bf16[2,32,32,768]{3,2,0,1:T(8,128)(2,1)} %copy.63), calls=%async_computation | async-start | bytes 6291456 | tf_op jit(solution)/shard_map/all_to_all | solution.py:49
  57.6 5.4 %copy-start.5 = (f32[512,2]{0,1:T(2,128)S(1)}, f32[512,2]{0,1:T(2,128)}, u32[]{:S(2)}) copy-start(f32[512,2]{0,1:T(2,128)} %param.8) | copy-start | bytes 12292
  77.7 45.0 %all-to-all-start.2 = ((bf16[2,32,32,768]{3,2,0,1:T(8,128)(2,1)}), bf16[2,32,32,768]{3,2,0,1:T(8,128)(2,1)}, u32[]{:S(2)}, u32[]{:S(2)}) async-start(bf16[2,32,32,768]{3,2,0,1:T(8,128)(2,1)} %copy.73), calls=%async_computation.4 | async-start | bytes 6291456 | tf_op jit(solution)/shard_map/all_to_all | solution.py:49
  82.7 90.3 %reduce-scatter.9.cloned.1.call-start = ((), (), s32[]{:S(2)}) async-start(), calls=%async_computation.10 | async-start | bytes 3932160 | tf_op jit(solution)/shard_map/reduce_scatter | solution.py:61
  83.0 2.8 copy-start.6
  83.2 1.7 copy-start.2
  122.6 2.6 copy-start.8
  124.9 6.9 %copy-start.1 = (bf16[2,32,32,768]{3,2,1,0:T(8,128)(2,1)}, bf16[2,32,32,768]{3,2,1,0:T(8,128)(2,1)S(1)}, u32[]{:S(2)}) copy-start(bf16[2,32,32,768]{3,2,1,0:T(8,128)(2,1)S(1)} %copy.74) | copy-start | bytes 9437188
  125.3 8.2 %copy-start.7 = (bf16[2,768,768]{2,1,0:T(8,128)(2,1)S(1)}, bf16[2,768,768]{2,1,0:T(8,128)(2,1)}, u32[]{:S(2)}) copy-start(bf16[2,768,768]{2,1,0:T(8,128)(2,1)} %param.10) | copy-start | bytes 7077892
  131.8 1.6 copy-start.10
  136.7 76.8 %reduce-scatter.11.cloned.1.call-start = ((), (), s32[]{:S(2)}) async-start(), calls=%async_computation.11 | async-start | bytes 3932160 | tf_op jit(solution)/shard_map/reduce_scatter | solution.py:61
  141.3 1.7 copy-start.9
  141.3 112.6 %reduce-scatter.5.cloned.1.call-start = ((), (), s32[]{:S(2)}) async-start(), calls=%async_computation.8 | async-start | bytes 3932160 | tf_op jit(solution)/shard_map/reduce_scatter | solution.py:61
  147.9 146.3 %reduce-scatter.7.cloned.1.call-start = ((), (), s32[]{:S(2)}) async-start(), calls=%async_computation.9 | async-start | bytes 3932160 | tf_op jit(solution)/shard_map/reduce_scatter | solution.py:61
  216.2 80.8 %all-to-all-start.3 = ((bf16[192,2,32,32]{0,3,1,2:T(8,128)(2,1)}), bf16[192,2,32,32]{0,3,1,2:T(8,128)(2,1)S(1)}, u32[]{:S(2)}, u32[]{:S(2)}) async-start(bf16[192,2,32,32]{0,3,1,2:T(8,128)(2,1)} %copy.77), calls=%async_computation.7 | async-start | bytes 2097152 | tf_op jit(solution)/shard_map/all_to_all | solution.py:72
  297.0 24.7 %all-to-all-start.1 = ((bf16[192,2,32,32]{0,3,1,2:T(8,128)(2,1)}), bf16[192,2,32,32]{0,3,1,2:T(8,128)(2,1)S(1)}, u32[]{:S(2)}, u32[]{:S(2)}) async-start(bf16[192,2,32,32]{0,3,1,2:T(8,128)(2,1)} %copy.67), calls=%async_computation.3 | async-start | bytes 2097152 | tf_op jit(solution)/shard_map/all_to_all | solution.py:72
  304.7 7.2 %copy-start = (pred[512,2,2048]{2,1,0:T(4,128)(4,1)S(1)}, pred[512,2,2048]{2,1,0:T(4,128)(4,1)}, u32[]{:S(2)}) copy-start(pred[512,2,2048]{2,1,0:T(4,128)(4,1)} %eq.58) | copy-start | bytes 6291460
Sparse Core Ops, SparseCore 0:
  136.8 36.2 reduce-scatter.8
  175.5 37.9 reduce-scatter.10
  215.9 37.9 reduce-scatter.4
  256.2 37.9 reduce-scatter.6
where the time goes:
time: 336 us; the launch traced here: 335 us
  waiting for transfers between devices  155 us (46%)
  matrix products  63.1 us (19%)
  local copies, waits for them, and re-layouts  37.5 us (11%)
  starting transfers between devices  31.5 us (9%)
  blocking collectives  25.9 us (8%)
  between operations  14.1 us (4%)
  other arithmetic  7.85 us (2%)
    reduce_scatter x4, waiting for transfers between devices, send_home(): lax.psum_scatter(with_layout_constraint(part, Layout((0, 1))), 'ffn', sca...  111 us
    all_to_all x2, waiting for transfers between devices, dispatch(): lax.all_to_all(send, 'expert', split_axis=1, concat_axis=1, tiled=True)  37.8 us
    all_to_all x2, starting transfers between devices, dispatch(): lax.all_to_all(send, 'expert', split_axis=1, concat_axis=1, tiled=True)  15.6 us
    all_to_all x2, starting transfers between devices, send_home(): lax.all_to_all(cols, 'expert', split_axis=2, concat_axis=2, tiled=True)  15.6 us
    all_gather x1, blocking collectives, shards(): whole_cot = lax.all_gather(cotangent, 'ffn', axis=1, tiled=True)  13 us
    all_gather x1, blocking collectives, shards(): whole_tokens = lax.all_gather(tokens, 'ffn', axis=1, tiled=True)  12.9 us
    dot_general x2, matrix products, gather_back(): lax.dot_general(placer, returned, (((0,), (1,)), ((), ())), preferred_ele...  10.7 us
    dot_general x2, matrix products, shards(): jnp.einsum('fd,sf->ds', down_weight[x], activated[x], preferred_element_t...  9.43 us
  transfers between devices with their start and end apart: 8, of which 7 were waited for; matrix products, arithmetic and copies ran while one was open for 23% of the time, Pallas kernels for 0%

commit v1 on v0

--- a/solution.py
+++ b/solution.py
@@ -3,6 +3,14 @@
 from jax import lax
 from jax.experimental.layout import Layout, with_layout_constraint
 from jax.sharding import PartitionSpec as P
+
+
+def tiled_gather(array, axis, dim):
+    size = lax.axis_size(axis)
+    repeats = [size if d == dim else 1 for d in range(array.ndim)]
+    return lax.all_to_all(
+        jnp.tile(array, repeats), axis, split_axis=dim, concat_axis=dim, tiled=True
+    )
 
 
 def slot_targets(expert_ids, owners, local_experts, capacity):
@@ -42,7 +50,7 @@
     )
     weights = gates.reshape(-1)
     whole_tokens = lax.all_gather(tokens, "ffn", axis=1, tiled=True)
-    whole_cot = lax.all_gather(cotangent, "ffn", axis=1, tiled=True)
+    whole_cot = tiled_gather(cotangent, "ffn", 1)
 
     def dispatch(send):
         send = send.astype(jnp.bfloat16).reshape(local_experts, owners, capacity, send.shape[1])

time: 336 us -> 300 us (0.89)
  waiting for transfers between devices: 155 us -> 63.6 us
  blocking collectives: 25.9 us -> 106 us
  starting transfers between devices: 31.5 us -> 16.1 us
  local copies, waits for them, and re-layouts: 37.5 us -> 32.1 us
  matrix products: 63.1 us -> 58.5 us
    all_to_all x0 -> x2, blocking collectives: none -> 93.4 us  [dispatch(): lax.all_to_all(send, 'expert', split_axis=1, concat_axis=1, tiled=True)]
    reduce_scatter x4, waiting for transfers between devices: 111 us -> 43.6 us  [send_home(): lax.psum_scatter(with_layout_constraint(part, Layout((0, 1))), 'ffn', sca...]
    all_to_all x2 -> x1, waiting for transfers between devices: 37.8 us -> 14.6 us  [tiled_gather(): lax.all_to_all(jnp.tile(array, repeats), axis, split_axis=dim, concat_axi...]
    all_gather x1 -> x0, blocking collectives: 13 us -> none  [shards(): whole_cot = lax.all_gather(cotangent, 'ffn', axis=1, tiled=True)]
    all_to_all x2 -> x1, starting transfers between devices: 15.6 us -> 4.13 us  [tiled_gather(): lax.all_to_all(jnp.tile(array, repeats), axis, split_axis=dim, concat_axi...]
    all_to_all x2, starting transfers between devices: 15.6 us -> 11.7 us  [send_home(): lax.all_to_all(cols, 'expert', split_axis=2, concat_axis=2, tiled=True)]
    unnamed x24 -> x30, local copies, waits for them, and re-layouts: 7.06 us -> 10.7 us
  transfers between devices with their start and end apart: 8 -> 7, of which waited for: 7 -> 4; matrix products, arithmetic and copies ran while one was open for 23% -> 23% of each run, Pallas kernels for 0% -> 0%
where the time goes in v1:
time: 300 us; the launch traced here: 299 us
  blocking collectives  106 us (35%)
  waiting for transfers between devices  63.6 us (21%)
  matrix products  58.5 us (20%)
  local copies, waits for them, and re-layouts  32.1 us (11%)
  starting transfers between devices  16.1 us (5%)
  between operations  14.1 us (5%)
  other arithmetic  8.13 us (3%)
    all_to_all x2, blocking collectives, dispatch(): lax.all_to_all(send, 'expert', split_axis=1, concat_axis=1, tiled=True)  93.4 us
    reduce_scatter x4, waiting for transfers between devices, send_home(): lax.psum_scatter(with_layout_constraint(part, Layout((0, 1))), 'ffn', sca...  43.6 us
    all_to_all x1, waiting for transfers between devices, tiled_gather(): lax.all_to_all(jnp.tile(array, repeats), axis, split_axis=dim, concat_axi...  14.6 us
    all_gather x1, blocking collectives, shards(): whole_tokens = lax.all_gather(tokens, 'ffn', axis=1, tiled=True)  12.9 us
    all_to_all x2, starting transfers between devices, send_home(): lax.all_to_all(cols, 'expert', split_axis=2, concat_axis=2, tiled=True)  11.7 us
    dot_general x2, matrix products, gather_back(): lax.dot_general(placer, returned, (((0,), (1,)), ((), ())), preferred_ele...  10.7 us
    unnamed x30, local copies, waits for them, and re-layouts  10.7 us
    dot_general x2, matrix products, shards(): jnp.einsum('fd,sf->ds', down_weight[x], activated[x], preferred_element_t...  8.38 us
  transfers between devices with their start and end apart: 7, of which 4 were waited for; matrix products, arithmetic and copies ran while one was open for 23% of the time, Pallas kernels for 0%

profile of v1, /device:TPU:1, one launch (start us, length us, event | category | flops | bytes accessed | tf_op | source)
XLA Modules:
  0.0 298.9 jit_solution(17932421227807978051)
XLA Ops:
  7.2 0.9 copy.55
  8.1 0.7 broadcast_compare_fusion
  8.8 0.2 reshape.157
  9.0 0.6 fusion.35
  9.6 0.2 convert_element_type.64
  9.8 0.2 copy.60
  10.0 0.3 fusion.38
  10.3 0.3 slice_reduce_fusion.1
  10.6 12.9 %all_gather.3 = bf16[512,768]{0,1:T(8,128)(2,1)S(1)} all-gather(bf16[512,192]{0,1:T(8,128)(2,1)S(1)} %copy-done.3), channel_id=1, replica_groups=mesh['expert'=32,'ffn'=4] {'ffn'}, dimensions={1}, use_global_device_ids=true | all-gather | bytes 983040 | tf_op jit(solution)/shard_map/all_gather | solution.py:52
  23.5 2.1 fusion.6
  25.5 0.3 copy.63
  25.8 49.5 %all_to_all.26 = bf16[2,32,32,768]{3,2,0,1:T(8,128)(2,1)S(1)} all-to-all(bf16[2,32,32,768]{3,2,0,1:T(8,128)(2,1)S(1)} %copy.63), channel_id=1, replica_groups=mesh['expert'=32,'ffn'=4] {'expert'}, dimensions={1} | all-to-all | bytes 6291456 | tf_op jit(solution)/shard_map/all_to_all | solution.py:57
  75.4 0.2 copy.64
  75.6 2.5 copy-done.8
  78.1 5.1 %multiply_convert_fusion.1 = (bf16[2,1024,768]{2,1,0:T(8,128)(2,1)S(1)}, f32[2,1024,768]{2,1,0:T(8,128)}) fusion(bf16[2,1024,768]{2,1,0:T(8,128)(2,1)S(1)} %bitcast.60, bf16[2,768,768]{2,1,0:T(8,128)(2,1)S(1)} %copy-done.8), kind=kOutput, calls=%fused_computation.4 | convolution fusion | flops 2423783424 | bytes 14942208 | tf_op jit(solution)/shard_map/xsd,xdf->xsf/dot_general | solution.py:83
  83.2 1.6 copy-done.11
  84.9 3.1 %convolution_bitcast_fusion.3 = f32[768,1024]{1,0:T(8,128)} fusion(bf16[2,1024,768]{2,1,0:T(8,128)(2,1)S(1)} %get-tuple-element.6, bf16[2,768,768]{2,1,0:T(8,128)(2,1)S(1)} %copy-done.6), kind=kOutput, calls=%fused_computation.27 | convolution fusion | flops 1207959552 | bytes 5898240 | tf_op jit(solution)/shard_map/fd,sf->ds/dot_general | solution.py:87
  88.0 0.9 copy-done.4
  88.9 0.9 tile.2
  89.8 4.1 %all-to-all-start.2 = ((bf16[512,4,192]{0,2,1:T(8,128)(2,1)}), bf16[512,4,192]{0,2,1:T(8,128)(2,1)S(1)}, u32[]{:S(2)}, u32[]{:S(2)}) async-start(bf16[512,4,192]{0,2,1:T(8,128)(2,1)} %tile.2), calls=%async_computation.4 | async-start | bytes 1572864 | tf_op jit(solution)/shard_map/all_to_all | solution.py:11
  93.9 5.3 %convolution_bitcast_fusion.2 = f32[768,1024]{1,0:T(8,128)} fusion(bf16[2,1024,768]{2,1,0:T(8,128)(2,1)} %copy-done.11, bf16[2,768,768]{2,1,0:T(8,128)(2,1)} %param.11), kind=kOutput, calls=%fused_computation.26 | convolution fusion | flops 1207959552 | bytes 5898240 | tf_op jit(solution)/shard_map/fd,sf->ds/dot_general | solution.py:87
  99.3 0.2 reduce-scatter.9.cloned.1.call-start
  99.5 0.4 copy-done.5
  99.9 0.1 copy.71
  100.1 0.2 mul.75
  100.3 14.6 %all-to-all-done.2 = bf16[512,4,192]{0,2,1:T(8,128)(2,1)S(1)} async-done(((bf16[512,4,192]{0,2,1:T(8,128)(2,1)}), bf16[512,4,192]{0,2,1:T(8,128)(2,1)S(1)}, u32[]{:S(2)}, u32[]{:S(2)}) %all-to-all-start.2) | async-done | bytes 786464 | tf_op jit(solution)/shard_map/all_to_all | solution.py:11
  114.8 0.3 bitcast_convert_fusion
  115.1 1.6 copy.72
  116.7 2.5 broadcast_in_dim.2
  119.2 3.4 %convert_element_type.70 = f32[1024,768]{1,0:T(8,128)} reshape(f32[512,2,768]{2,1,0:T(2,128)S(1)} %broadcast_in_dim.2) | data formatting | bytes 6291456 | tf_op jit(solution)/shard_map/convert_element_type | solution.py:61
  122.6 6.0 %fusion.9 = bf16[2048,768]{1,0:T(8,128)(2,1)S(1)} fusion(s32[1024]{0:T(1024)S(1)} %fusion.48, f32[1024,768]{1,0:T(8,128)} %convert_element_type.70, f32[1024]{0:T(1024)S(1)} %mul.75), kind=kOutput, calls=%fused_computation.14 | convolution fusion | flops 3226468352 | bytes 6299648 | tf_op jit(solution)/shard_map/dot_general | solution.py:64
  128.7 0.3 copy.73
  129.0 43.8 %all_to_all.27 = bf16[2,32,32,768]{3,2,0,1:T(8,128)(2,1)S(1)} all-to-all(bf16[2,32,32,768]{3,2,0,1:T(8,128)(2,1)S(1)} %copy.73), channel_id=1, replica_groups=mesh['expert'=32,'ffn'=4] {'expert'}, dimensions={1} | all-to-all | bytes 6291456 | tf_op jit(solution)/shard_map/all_to_all | solution.py:57
  172.8 0.2 copy.74
  173.1 2.5 copy-done.7
  175.6 3.8 %multiply_convert_fusion = bf16[2,1024,768]{2,1,0:T(8,128)(2,1)S(1)} fusion(f32[2,1024,768]{2,1,0:T(8,128)S(1)} %bitcast.73, bf16[2,1024,768]{2,1,0:T(8,128)(2,1)S(1)} %bitcast.62, bf16[2,768,768]{2,1,0:T(8,128)(2,1)S(1)} %copy-done.7), kind=kOutput, calls=%fused_computation.3 | convolution fusion | flops 2430074880 | bytes 14942208 | tf_op jit(solution)/shard_map/xsd,xfd->xsf/dot_general | solution.py:91
  179.4 1.6 copy-done.10
  181.0 3.2 %convolution_bitcast_fusion.1 = f32[768,1024]{1,0:T(8,128)} fusion(bf16[2,1024,768]{2,1,0:T(8,128)(2,1)S(1)} %multiply_convert_fusion, bf16[2,768,768]{2,1,0:T(8,128)(2,1)S(1)} %copy-done.9), kind=kOutput, calls=%fused_computation.25 | convolution fusion | flops 1207959552 | bytes 5898240 | tf_op jit(solution)/shard_map/df,sf->ds/dot_general | solution.py:102
  184.3 4.6 %convolution_bitcast_fusion = f32[768,1024]{1,0:T(8,128)} fusion(bf16[2,1024,768]{2,1,0:T(8,128)(2,1)} %copy-done.10, bf16[2,768,768]{2,1,0:T(8,128)(2,1)S(1)} %copy-done.9), kind=kOutput, calls=%fused_computation.24 | convolution fusion | flops 1207959552 | bytes 5898240 | tf_op jit(solution)/shard_map/df,sf->ds/dot_general | solution.py:102
  188.9 1.7 iota_compare_fusion.1
  190.6 7.8 %eq.58 = pred[512,2,2048]{2,1,0:T(4,128)(4,1)} reshape(pred[1024,2048]{1,0:T(8,128)(4,1)S(1)} %iota_compare_fusion.1) | data formatting | bytes 4194304 | tf_op jit(solution)/shard_map/eq | solution.py:45
  198.4 1.2 convert.17
  199.6 0.2 copy.65
  199.8 1.2 convert.18
  201.0 0.2 copy.66
  201.2 0.2 pad_maximum_fusion
  201.5 1.1 copy.67
  202.5 4.0 %all-to-all-start.1 = ((bf16[192,2,32,32]{0,3,1,2:T(8,128)(2,1)}), bf16[192,2,32,32]{0,3,1,2:T(8,128)(2,1)S(1)}, u32[]{:S(2)}, u32[]{:S(2)}) async-start(bf16[192,2,32,32]{0,3,1,2:T(8,128)(2,1)} %copy.67), calls=%async_computation.3 | async-start | bytes 2097152 | tf_op jit(solution)/shard_map/all_to_all | solution.py:80
  206.5 7.0 %convolution_convert_fusion.1 = bf16[2,768,768]{2,1,0:T(8,128)(2,1)} fusion(bf16[2,1024,768]{2,1,0:T(8,128)(2,1)} %bitcast.61, bf16[2,1024,768]{2,1,0:T(8,128)(2,1)} %copy-done.10), kind=kOutput, calls=%fused_computation.23 | convolution fusion | flops 2417098752 | bytes 8650752 | tf_op jit(solution)/shard_map/xsd,xsf->xdf/dot_general | solution.py:98
  213.5 4.7 %reduce-scatter.9.cloned.1.call-done = f32[192,1024]{1,0:T(8,128)} async-done(((f32[768,1024]{1,0:T(8,128)}), f32[192,1024]{1,0:T(8,128)}) %reduce-scatter.9.cloned.1.call-update) | async-done | bytes 786448 | tf_op jit(solution)/shard_map/reduce_scatter | solution.py:69
  218.2 1.2 convert.19
  219.4 0.2 copy.75
  219.6 38.9 %reduce-scatter.11.cloned.1.call-done = f32[192,1024]{1,0:T(8,128)} async-done(((f32[768,1024]{1,0:T(8,128)}), f32[192,1024]{1,0:T(8,128)}) %reduce-scatter.11.cloned.1.call-update) | async-done | bytes 786448 | tf_op jit(solution)/shard_map/reduce_scatter | solution.py:69
  258.5 1.2 convert.20
  259.7 0.2 copy.76
  259.9 0.2 pad_maximum_fusion.1
  260.1 1.1 copy.77
  261.2 7.8 %all-to-all-start.4 = ((bf16[192,2,32,32]{0,3,1,2:T(8,128)(2,1)}), bf16[192,2,32,32]{0,3,1,2:T(8,128)(2,1)S(1)}, u32[]{:S(2)}, u32[]{:S(2)}) async-start(bf16[192,2,32,32]{0,3,1,2:T(8,128)(2,1)} %copy.77), calls=%async_computation.8 | async-start | bytes 2097152 | tf_op jit(solution)/shard_map/all_to_all | solution.py:80
  269.0 7.1 %convolution_convert_fusion = bf16[2,768,768]{2,1,0:T(8,128)(2,1)} fusion(bf16[2,1024,768]{2,1,0:T(8,128)(2,1)} %copy-done.11, bf16[2,1024,768]{2,1,0:T(8,128)(2,1)} %bitcast.63), kind=kOutput, calls=%fused_computation.22 | convolution fusion | flops 2417098752 | bytes 8650752 | tf_op jit(solution)/shard_map/xsf,xsd->xfd/dot_general | solution.py:95
  276.1 0.1 copy.68
  276.2 4.3 %fusion.20 = bf16[512,192]{0,1:T(8,128)(2,1)} fusion(bf16[192,2048,1]{0,1,2:T(8,128)(2,1)S(1)} %bitcast.71, pred[512,2,2048]{2,1,0:T(4,128)(4,1)S(1)} %copy-done, f32[512,2]{0,1:T(2,128)S(1)} %copy-done.5), kind=kOutput, calls=%fused_computation.34 | convolution fusion | flops 805601280 | bytes 3084288 | tf_op jit(solution)/shard_map/dot_general | solution.py:108
  280.4 5.4 %all-to-all-done.4 = bf16[192,2,32,32]{0,3,1,2:T(8,128)(2,1)S(1)} async-done(((bf16[192,2,32,32]{0,3,1,2:T(8,128)(2,1)}), bf16[192,2,32,32]{0,3,1,2:T(8,128)(2,1)S(1)}, u32[]{:S(2)}, u32[]{:S(2)}) %all-to-all-start.4) | async-done | bytes 786464 | tf_op jit(solution)/shard_map/all_to_all | solution.py:80
  285.9 0.1 copy.78
  285.9 6.4 %fusion.23 = bf16[512,192]{0,1:T(8,128)(2,1)} fusion(bf16[192,2048,1]{0,1,2:T(8,128)(2,1)S(1)} %bitcast.70, pred[512,2,2048]{2,1,0:T(4,128)(4,1)} %eq.58), kind=kOutput, calls=%fused_computation.35 | convolution fusion | flops 805404672 | bytes 3080192 | tf_op jit(solution)/shard_map/dot_general | solution.py:108
  (35 shorter events, 0.2 us)
Async XLA Ops:
  7.2 3.4 %copy-start.3 = (bf16[512,192]{0,1:T(8,128)(2,1)S(1)}, bf16[512,192]{0,1:T(8,128)(2,1)}, u32[]{:S(2)}) copy-start(bf16[512,192]{0,1:T(8,128)(2,1)} %param.6) | copy-start | bytes 589828
  7.2 191.2 %reduce-scatter.5.cloned.1.call-start = ((), (), s32[]{:S(2)}) async-start(), calls=%async_computation.9 | async-start | bytes 3932160 | tf_op jit(solution)/shard_map/reduce_scatter | solution.py:69
  75.4 2.8 copy-start.8
  75.6 7.6 %copy-start.1 = (bf16[2,32,32,768]{3,2,1,0:T(8,128)(2,1)}, bf16[2,32,32,768]{3,2,1,0:T(8,128)(2,1)S(1)}, u32[]{:S(2)}) copy-start(bf16[2,32,32,768]{3,2,1,0:T(8,128)(2,1)S(1)} %copy.64) | copy-start | bytes 9437188
  78.1 6.7 %copy-start.6 = (bf16[2,768,768]{2,1,0:T(8,128)(2,1)S(1)}, bf16[2,768,768]{2,1,0:T(8,128)(2,1)}, u32[]{:S(2)}) copy-start(bf16[2,768,768]{2,1,0:T(8,128)(2,1)} %param.11) | copy-start | bytes 7077892
  83.2 1.6 copy-start.11
  87.9 0.9 copy-start.4
  89.8 25.0 %all-to-all-start.2 = ((bf16[512,4,192]{0,2,1:T(8,128)(2,1)}), bf16[512,4,192]{0,2,1:T(8,128)(2,1)S(1)}, u32[]{:S(2)}, u32[]{:S(2)}) async-start(bf16[512,4,192]{0,2,1:T(8,128)(2,1)} %tile.2), calls=%async_computation.4 | async-start | bytes 1572864 | tf_op jit(solution)/shard_map/all_to_all | solution.py:11
  93.9 105.9 %reduce-scatter.7.cloned.1.call-start = ((), (), s32[]{:S(2)}) async-start(), calls=%async_computation.10 | async-start | bytes 3932160 | tf_op jit(solution)/shard_map/reduce_scatter | solution.py:69
  99.2 0.7 copy-start.5
  99.3 118.9 %reduce-scatter.9.cloned.1.call-start = ((), (), s32[]{:S(2)}) async-start(), calls=%async_computation.11 | async-start | bytes 3932160 | tf_op jit(solution)/shard_map/reduce_scatter | solution.py:69
  128.7 44.4 %slice-start = ((s8[6291456]{0:T(1024)(128)(4,1)}), s8[4194304]{0:T(1024)(128)(4,1)S(1)}, s32[]{:S(2)}) async-start(s8[6291456]{0:T(1024)(128)(4,1)} %bitcast.72), calls=%async_computation.13 | async-start | bytes 8388608
  129.0 44.1 %slice-start.1 = ((s8[6291456]{0:T(1024)(128)(4,1)}), s8[2097152]{0:T(1024)(128)(4,1)S(1)}, s32[]{:S(2)}) async-start(s8[6291456]{0:T(1024)(128)(4,1)} %bitcast.72), calls=%async_computation.14 | async-start | bytes 4194304
  172.8 2.8 copy-start.7
  173.0 6.4 %copy-start.2 = (bf16[2,32,32,768]{3,2,1,0:T(8,128)(2,1)}, bf16[2,32,32,768]{3,2,1,0:T(8,128)(2,1)S(1)}, u32[]{:S(2)}) copy-start(bf16[2,32,32,768]{3,2,1,0:T(8,128)(2,1)S(1)} %copy.74) | copy-start | bytes 9437188
  175.6 5.5 %copy-start.9 = (bf16[2,768,768]{2,1,0:T(8,128)(2,1)S(1)}, bf16[2,768,768]{2,1,0:T(8,128)(2,1)}, u32[]{:S(2)}) copy-start(bf16[2,768,768]{2,1,0:T(8,128)(2,1)} %param.10) | copy-start | bytes 7077892
  179.4 1.6 copy-start.10
  184.2 74.3 %reduce-scatter.11.cloned.1.call-start = ((), (), s32[]{:S(2)}) async-start(), calls=%async_computation.12 | async-start | bytes 3932160 | tf_op jit(solution)/shard_map/reduce_scatter | solution.py:69
  202.5 58.7 %all-to-all-start.1 = ((bf16[192,2,32,32]{0,3,1,2:T(8,128)(2,1)}), bf16[192,2,32,32]{0,3,1,2:T(8,128)(2,1)S(1)}, u32[]{:S(2)}, u32[]{:S(2)}) async-start(bf16[192,2,32,32]{0,3,1,2:T(8,128)(2,1)} %copy.67), calls=%async_computation.3 | async-start | bytes 2097152 | tf_op jit(solution)/shard_map/all_to_all | solution.py:80
  261.2 24.7 %all-to-all-start.4 = ((bf16[192,2,32,32]{0,3,1,2:T(8,128)(2,1)}), bf16[192,2,32,32]{0,3,1,2:T(8,128)(2,1)S(1)}, u32[]{:S(2)}, u32[]{:S(2)}) async-start(bf16[192,2,32,32]{0,3,1,2:T(8,128)(2,1)} %copy.77), calls=%async_computation.8 | async-start | bytes 2097152 | tf_op jit(solution)/shard_map/all_to_all | solution.py:80
  269.0 7.2 %copy-start = (pred[512,2,2048]{2,1,0:T(4,128)(4,1)S(1)}, pred[512,2,2048]{2,1,0:T(4,128)(4,1)}, u32[]{:S(2)}) copy-start(pred[512,2,2048]{2,1,0:T(4,128)(4,1)} %eq.58) | copy-start | bytes 6291460
Sparse Core Ops, SparseCore 0:
  88.1 44.3 reduce-scatter.4
  134.9 34.7 reduce-scatter.6
  184.3 33.8 reduce-scatter.8
  220.5 37.9 reduce-scatter.10
